TPU v7x, 256 devices: a whole 4x4x8 slice. The times are simulated.
256 devices in a mesh: wide: 64 (over y, z, core), col: 4 (over x).
Axes of the slice: x: 4, y: 4, z: 8, core: 2. Of those that a mesh axis runs over, the one named last changes fastest.
Arguments:
- assembled: float32 [9216, 1024], P(('wide', 'col')), as said below
- row_map: int32 [9216], P(('wide', 'col')), may hold values from 0 to 9215, as said below
- fill_pattern: int32 [2, 32], replicated, may hold values from 0 to 1
- trailing_block: float32 [64, 4, 32, 8192], P(None, 'col', None, 'wide'), may hold values from -6 to 6
Outputs:
- schur: float32 [64, 4, 32, 8192], P(None, 'col', None, 'wide')
- panel_rows: float32 [8192, 1024], P(('wide', 'col'))
- diag_factor: float32 [1024, 1024], P(('wide', 'col'))
Inputs may be any that keep to these rules, and one draw needn't show every extreme that they name: row_map is a permutation of the window rows. Each device, with col index c, holds exactly 32 trailing rows 1024 + t whose owner device index t // 32 has col index c, and exactly 4 rows d below 1024 with d // 256 equal to c. At most 2 of one device's trailing rows have the same owner, and every device holds exactly 2 trailing rows of some owner. `assembled`: D is symmetric positive definite.
All inputs are finite; a program needn't handle non-finite values.
Results may differ from a plain program's by a relative error of at most 0.00008.
Values sent between devices are 32-bit elements; how exact they have to be, the bound alone decides.
No kernel may reach another device: no remote copies, remote signals or barrier semaphores. Data moves between devices by JAX's collectives and lax.ppermute only.
A program may use at most 128 MiB of HBM per device.

v0:
```python
import jax
import jax.numpy as jnp
from jax import lax
from jax.sharding import PartitionSpec as P

BLOCK = 256
highest = lax.Precision.HIGHEST


def lower_inverse(lower_factor):
    order_size = lower_factor.shape[0]
    identity = jnp.eye(order_size, dtype=lower_factor.dtype)
    return lax.linalg.triangular_solve(lower_factor, identity, left_side=True, lower=True)


def contract_rows(left_rows, right_rows):
    return lax.dot_general(left_rows, right_rows, (((1,), (1,)), ((), ())), precision=highest)


def local(assembled, row_map, fill_pattern, trailing_block):
    wide_count = lax.axis_size("wide")
    col_count = lax.axis_size("col")
    asm_rows, twice_width = assembled.shape
    half_width = twice_width // 2
    trail_rows = trailing_block.shape[2]
    diag_share = twice_width // (col_count * wide_count)
    diag_col = twice_width // col_count
    wide_index = lax.axis_index("wide")
    col_index = lax.axis_index("col")
    device_index = wide_index * col_count + col_index
    packed_rows = (asm_rows + 1 + 7) // 8 * 8
    id_row = jnp.zeros((twice_width,), jnp.float32).at[:asm_rows].set(row_map.astype(jnp.float32))
    packed = jnp.concatenate(
        [
            assembled,
            id_row[None, :],
            jnp.zeros((packed_rows - asm_rows - 1, twice_width), jnp.float32),
        ],
        axis=0,
    )
    gathered = lax.all_gather(packed, "wide", axis=0, tiled=True)
    gathered3 = gathered.reshape(wide_count, packed_rows, twice_width)
    ids = gathered3[:, asm_rows, :asm_rows].astype(jnp.int32).reshape(-1)
    source = (
        jnp.arange(wide_count)[:, None] * packed_rows + jnp.arange(asm_rows)[None, :]
    ).reshape(-1)
    is_diagonal = ids < twice_width
    diag_slot = jnp.where(is_diagonal, ids - diag_col * col_index, diag_col)
    diag_src = jnp.zeros((diag_col,), jnp.int32).at[diag_slot].set(source, mode="drop")
    diag_block = gathered[diag_src]
    full = lax.all_gather(diag_block, "col", axis=0, tiled=True)
    trail_id = ids - twice_width
    owner_wide = trail_id // (trail_rows * col_count)
    trail_slot = jnp.where(
        is_diagonal, wide_count * trail_rows, owner_wide * trail_rows + trail_id % trail_rows
    )
    trail_src = (
        jnp.zeros((wide_count * trail_rows,), jnp.int32).at[trail_slot].set(source, mode="drop")
    )
    trail_all = gathered[trail_src]
    row_global = (
        (jnp.arange(wide_count)[:, None] * col_count + col_index) * trail_rows
        + jnp.arange(trail_rows)[None, :]
    ).reshape(-1)
    block_ids = row_global // BLOCK
    first_flags = fill_pattern[0][block_ids]
    second_flags = fill_pattern[1][block_ids]
    column_first = jnp.arange(twice_width) < half_width
    keep = jnp.where(column_first[None, :], first_flags[:, None], second_flags[:, None]).astype(
        jnp.float32
    )
    masked_all = trail_all * keep
    masked_own = lax.dynamic_slice_in_dim(masked_all, wide_index * trail_rows, trail_rows, 0)
    masked_range = lax.all_gather(masked_own, "col", axis=0, tiled=True)
    symmetric = (full + full.T) * 0.5
    factor = jnp.linalg.cholesky(symmetric)
    inverse = lower_inverse(factor)
    panel = contract_rows(masked_own, inverse)
    range_panel = contract_rows(masked_range, inverse)
    range_back = lax.dot_general(range_panel, inverse, (((1,), (0,)), ((), ())), precision=highest)
    update = contract_rows(masked_all, range_back)
    schur = trailing_block - update.reshape(trailing_block.shape)
    factor_rows = lax.dynamic_slice_in_dim(factor, device_index * diag_share, diag_share, 0)
    return (schur, panel, factor_rows)


def solution(mesh):
    in_specs = (P(("wide", "col"), None), P(("wide", "col")), P(), P(None, "col", None, "wide"))
    out_specs = (P(None, "col", None, "wide"), P(("wide", "col"), None), P(("wide", "col"), None))
    return jax.shard_map(local, mesh=mesh, in_specs=in_specs, out_specs=out_specs, check_vma=False)
```

profile of v0, /device:TPU:2, one launch (start us, length us, event | category | flops | bytes accessed | tf_op | source)
XLA Modules:
  0.0 598.0 jit_solution(17203450287779156365)
XLA Ops:
  7.9 1.7 fusion.50
  9.9 90.4 %all-gather.4.cloned.1.call-done = f32[2560,1024]{1,0:T(8,128)} async-done(((f32[40,1024]{1,0:T(8,128)}), f32[2560,1024]{1,0:T(8,128)}) %all-gather.4.cloned.1.call-update) | async-done | bytes 10485776 | tf_op jit(solution)/shard_map/all_gather | solution.py:41
  101.8 9.0 %scatter_custom_fusion.1 = s32[256]{0:T(256)S(1)} fusion(s32[2304]{0:T(1024)S(1)} %get-tuple-element.23, s32[2304]{0:T(1024)S(1)} %reshape.468, s32[]{:T(128)} %copy.61), kind=kCustom, calls=%fused_computation.238 | custom fusion | bytes 1028 | tf_op jit(solution)/shard_map/scatter | solution.py:49
  110.8 5.6 gather_fusion.1
  120.8 4.6 compare_select_fusion.7
  126.3 2.5 fusion.23
  128.8 4.2 compare_select_fusion.8
  133.1 15.6 %select_select_fusion.1 = s32[2048]{0:T(1024)S(1)} fusion(pred[2048]{0:T(1024)(128)(4,1)S(1)} %get-tuple-element.49, pred[2048]{0:T(1024)(128)(4,1)S(1)} %get-tuple-element.48, pred[2048]{0:T(1024)(128)(4,1)S(1)} %get-tuple-element.47, pred[2048]{0:T(1024)(128)(4,1)S(1)} %get-tuple-element.46, pred[2048]{0:T(1024)(128)(4,1)S(1)} %get-tuple-element.45, ...), kind=kLoop, calls=%fused_computation.212 | loop fusion | flops 51200 | bytes 67684 | tf_op jit(solution)/shard_map/gather | solution.py:67
  148.7 15.4 %select_select_fusion.2 = s32[2048]{0:T(1024)S(1)} fusion(pred[2048]{0:T(1024)(128)(4,1)S(1)} %get-tuple-element.49, pred[2048]{0:T(1024)(128)(4,1)S(1)} %get-tuple-element.48, pred[2048]{0:T(1024)(128)(4,1)S(1)} %get-tuple-element.47, pred[2048]{0:T(1024)(128)(4,1)S(1)} %get-tuple-element.46, pred[2048]{0:T(1024)(128)(4,1)S(1)} %get-tuple-element.45, ...), kind=kLoop, calls=%fused_computation.213 | loop fusion | flops 51200 | bytes 67684 | tf_op jit(solution)/shard_map/gather | solution.py:66
  164.2 9.0 %scatter_custom_fusion = s32[2048]{0:T(1024)S(1)} fusion(s32[2304]{0:T(1024)S(1)} %get-tuple-element.24, s32[2304]{0:T(1024)S(1)} %reshape.468, s32[]{:T(128)} %copy.61), kind=kCustom, calls=%fused_computation.216 | custom fusion | bytes 8196 | tf_op jit(solution)/shard_map/scatter | solution.py:58
  173.2 15.7 %gather_fusion = f32[2048,1024]{1,0:T(8,128)} fusion(f32[2560,1024]{1,0:T(8,128)} %all-gather.4.cloned.1.call-done, s32[2048]{0:T(1024)S(1)} %fusion.75), kind=kCustom, calls=%fused_computation | custom fusion | bytes 16785408 | tf_op jit(solution)/shard_map/gather | solution.py:60
  188.9 5.4 convert_multiply_fusion
  194.3 3.2 copy-done
  197.6 13.4 %all_gather.10 = f32[128,1024]{1,0:T(8,128)S(1)} all-gather(f32[32,1024]{1,0:T(8,128)S(1)} %constant_dynamic-slice_fusion.2), channel_id=1, replica_groups=mesh['wide'=64,'col'=4] {'col'}, dimensions={0}, use_global_device_ids=true | all-gather | bytes 655360 | tf_op jit(solution)/shard_map/all_gather | solution.py:74
  210.9 5.4 copy.13
  216.3 6.8 %fusion.1 = f32[1024,1024]{1,0:T(8,128)} fusion(f32[1024,1024]{1,0:T(8,128)} %copy.13, f32[1024,1024]{0,1:T(8,128)} %all-gather.6.cloned.1.call-done), kind=kLoop, calls=%fused_computation.10 | loop fusion | flops 2097152 | bytes 12582912 | tf_op jit(solution)/shard_map/mul | solution.py:75
  223.2 5.5 copy.14
  228.7 4.4 fusion
  233.1 2.0 copy-done.2
  235.1 11.7 %cholesky.223 = f32[128,128]{1,0:T(8,128)S(1)} custom-call(f32[128,128]{1,0:T(8,128)S(1)} %cholesky.580), custom_call_target="Cholesky" | custom-call | tf_op jit(solution)/shard_map/jit(cholesky)/cholesky | solution.py:76
  246.9 2.5 cholesky.255
  249.3 9.8 %custom-call.62 = f32[1,128,128]{1,2,0:T(8,128)S(1)} custom-call(f32[1,128,128]{2,1,0:T(8,128)S(1)} %get-tuple-element.110), custom_call_target="InvertDiagBlocksLowerTriangular" | custom-call | tf_op jit(solution)/shard_map/jit(cholesky)/cholesky | solution.py:76
  259.1 2.3 constant_dynamic-update-slice_fusion.30
  263.0 12.1 %cholesky.244 = f32[128,128]{1,0:T(8,128)S(1)} custom-call(f32[128,128]{1,0:T(8,128)S(1)} %cholesky.584), custom_call_target="Cholesky" | custom-call | tf_op jit(solution)/shard_map/jit(cholesky)/cholesky | solution.py:76
  275.8 9.8 %custom-call.63 = f32[1,128,128]{1,2,0:T(8,128)S(1)} custom-call(f32[1,128,128]{2,1,0:T(8,128)S(1)} %get-tuple-element.107), custom_call_target="InvertDiagBlocksLowerTriangular" | custom-call | tf_op jit(solution)/shard_map/jit(cholesky)/cholesky | solution.py:76
  286.9 2.1 convolution_subtract_fusion.6
  289.0 11.7 %cholesky.468 = f32[128,128]{1,0:T(8,128)S(1)} custom-call(f32[128,128]{1,0:T(8,128)S(1)} %cholesky.589), custom_call_target="Cholesky" | custom-call | tf_op jit(solution)/shard_map/jit(cholesky)/cholesky | solution.py:76
  302.0 9.8 %custom-call.64 = f32[1,128,128]{1,2,0:T(8,128)S(1)} custom-call(f32[1,128,128]{2,1,0:T(8,128)S(1)} %get-tuple-element.104), custom_call_target="InvertDiagBlocksLowerTriangular" | custom-call | tf_op jit(solution)/shard_map/jit(cholesky)/cholesky | solution.py:76
  313.0 2.3 convolution_subtract_fusion.7
  315.4 11.8 %cholesky.487 = f32[128,128]{1,0:T(8,128)S(1)} custom-call(f32[128,128]{1,0:T(8,128)S(1)} %cholesky.594), custom_call_target="Cholesky" | custom-call | tf_op jit(solution)/shard_map/jit(cholesky)/cholesky | solution.py:76
  328.5 9.8 %custom-call.65 = f32[1,128,128]{1,2,0:T(8,128)S(1)} custom-call(f32[1,128,128]{2,1,0:T(8,128)S(1)} %get-tuple-element.101), custom_call_target="InvertDiagBlocksLowerTriangular" | custom-call | tf_op jit(solution)/shard_map/jit(cholesky)/cholesky | solution.py:76
  339.4 2.3 convolution_subtract_fusion.8
  341.8 11.7 %cholesky.506 = f32[128,128]{1,0:T(8,128)S(1)} custom-call(f32[128,128]{1,0:T(8,128)S(1)} %cholesky.599), custom_call_target="Cholesky" | custom-call | tf_op jit(solution)/shard_map/jit(cholesky)/cholesky | solution.py:76
  354.8 10.0 %custom-call.66 = f32[1,128,128]{1,2,0:T(8,128)S(1)} custom-call(f32[1,128,128]{2,1,0:T(8,128)S(1)} %get-tuple-element.98), custom_call_target="InvertDiagBlocksLowerTriangular" | custom-call | tf_op jit(solution)/shard_map/jit(cholesky)/cholesky | solution.py:76
  365.8 2.3 convolution_subtract_fusion.9
  368.1 11.7 %cholesky.526 = f32[128,128]{1,0:T(8,128)S(1)} custom-call(f32[128,128]{1,0:T(8,128)S(1)} %cholesky.604), custom_call_target="Cholesky" | custom-call | tf_op jit(solution)/shard_map/jit(cholesky)/cholesky | solution.py:76
  381.1 9.8 %custom-call.67 = f32[1,128,128]{1,2,0:T(8,128)S(1)} custom-call(f32[1,128,128]{2,1,0:T(8,128)S(1)} %get-tuple-element.95), custom_call_target="InvertDiagBlocksLowerTriangular" | custom-call | tf_op jit(solution)/shard_map/jit(cholesky)/cholesky | solution.py:76
  391.9 2.1 convolution_subtract_fusion.10
  394.0 12.1 %cholesky.546 = f32[128,128]{1,0:T(8,128)S(1)} custom-call(f32[128,128]{1,0:T(8,128)S(1)} %cholesky.609), custom_call_target="Cholesky" | custom-call | tf_op jit(solution)/shard_map/jit(cholesky)/cholesky | solution.py:76
  407.4 9.8 %custom-call.68 = f32[1,128,128]{1,2,0:T(8,128)S(1)} custom-call(f32[1,128,128]{2,1,0:T(8,128)S(1)} %get-tuple-element.92), custom_call_target="InvertDiagBlocksLowerTriangular" | custom-call | tf_op jit(solution)/shard_map/jit(cholesky)/cholesky | solution.py:76
  418.1 1.8 convolution_subtract_fusion.11
  419.8 11.7 %cholesky.564 = f32[128,128]{1,0:T(8,128)S(1)} custom-call(f32[128,128]{1,0:T(8,128)S(1)} %convolution_subtract_fusion.11), custom_call_target="Cholesky" | custom-call | tf_op jit(solution)/shard_map/jit(cholesky)/cholesky | solution.py:76
  438.5 6.6 %fusion.2 = (f32[1024,1024]{1,0:T(8,128)}, f32[1024,1024]{1,0:T(8,128)}) fusion(f32[1024,1024]{1,0:T(8,128)} %get-tuple-element.90, pred[]{:T(512)S(6)} %cholesky.579), kind=kLoop, calls=%fused_computation.14 | loop fusion | flops 4194304 | bytes 12582913 | tf_op jit(solution)/shard_map/triangular_solve | solution.py:13
  445.1 23.2 %while.2 = (s32[]{:T(128)}, f32[1024,1024]{1,0:T(8,128)}, s32[8,2]{0,1:T(2,128)S(1)}, f32[8,128,128]{2,1,0:T(8,128)S(1)}, s32[]{:T(128)}) while((s32[]{:T(128)}, f32[1024,1024]{1,0:T(8,128)}, s32[8,2]{0,1:T(2,128)S(1)}, f32[8,128,128]{2,1,0:T(8,128)S(1)}, s32[]{:T(128)}) %tuple.153), condition=%wide.while_cond.1, body=%wide.while_body.1.sunk | while | flops 2 | bytes 131189 | solution.py:13
  445.7 2.3 bitcast_dynamic-update-slice_fusion.2
  448.6 2.3 bitcast_dynamic-update-slice_fusion.2
  451.5 2.3 bitcast_dynamic-update-slice_fusion.2
  454.4 2.3 bitcast_dynamic-update-slice_fusion.2
  457.3 2.3 bitcast_dynamic-update-slice_fusion.2
  460.2 2.3 bitcast_dynamic-update-slice_fusion.2
  463.1 2.3 bitcast_dynamic-update-slice_fusion.2
  466.0 2.2 bitcast_dynamic-update-slice_fusion.2
  468.3 78.8 %custom-call.69 = f32[8,128,128]{1,2,0:T(8,128)S(1)} custom-call(f32[8,128,128]{2,1,0:T(8,128)S(1)} %get-tuple-element.22), custom_call_target="InvertDiagBlocksLowerTriangular" | custom-call | tf_op jit(solution)/shard_map/triangular_solve | solution.py:13
  547.6 1.9 convolution_subtract_fusion.4
  550.3 1.6 convolution_subtract_fusion
  552.7 2.0 fusion.17
  555.5 2.2 fusion.20
  558.4 2.6 convolution_subtract_fusion.2
  561.8 2.8 convolution_subtract_fusion.1
  565.2 3.5 convolution_subtract_fusion.3
  569.4 4.6 fusion.91
  574.0 4.5 fusion.88
  578.4 2.4 fusion.89
  580.9 7.3 %fusion.90 = f32[2048,128]{1,0:T(8,128)S(1)} fusion(f32[2048,1024]{1,0:T(8,128)S(1)} %bitcast.196, f32[128,1024]{1,0:T(8,128)S(1)} %fusion.89), kind=kOutput, calls=%fused_computation.253 | convolution fusion | flops 3221225472 | bytes 9961472 | tf_op jit(solution)/shard_map/dot_general | solution.py:17
  (104 shorter events, 37.6 us)
Async XLA Ops:
  7.2 93.1 %all-gather.4.cloned.1.call-start = ((), (), s32[]{:S(2)}) async-start(), calls=%async_computation | async-start | bytes 10649600 | tf_op jit(solution)/shard_map/all_gather | solution.py:41
  9.6 201.3 %all-gather.6.cloned.1.call-start = ((), (), s32[]{:S(2)}) async-start(), calls=%async_computation.1 | async-start | bytes 5242880 | tf_op jit(solution)/shard_map/all_gather | solution.py:51
  110.8 7.1 %copy-start.4 = (s32[2,32]{1,0:T(2,128)S(1)}, s32[2,32]{1,0:T(2,128)}, u32[]{:S(2)}) copy-start(s32[2,32]{1,0:T(2,128)} %param.8) | copy-start | bytes 772
  194.3 3.2 copy-start
  233.1 2.0 copy-start.2
  547.0 3.2 copy-start.1
  568.7 12.1 %slice-start = ((s8[8388608]{0:T(1024)(128)(4,1)}), s8[4194304]{0:T(1024)(128)(4,1)S(1)}, s32[]{:S(2)}) async-start(s8[8388608]{0:T(1024)(128)(4,1)} %bitcast.195), calls=%async_computation.2 | async-start | bytes 8388608
  574.0 6.9 %slice-start.1 = ((s8[8388608]{0:T(1024)(128)(4,1)}), s8[4194304]{0:T(1024)(128)(4,1)S(1)}, s32[]{:S(2)}) async-start(s8[8388608]{0:T(1024)(128)(4,1)} %bitcast.195), calls=%async_computation.3 | async-start | bytes 8388608
  580.9 8.7 %copy-start.3 = (f32[64,1,32,128]{3,2,1,0:T(8,128)S(1)}, f32[64,1,32,128]{3,2,1,0:T(8,128)}, u32[]{:S(2)}) copy-start(f32[64,1,32,128]{3,2,1,0:T(8,128)} %param.9) | copy-start | bytes 3145732
Sparse Core Ops, SparseCore 0:
  11.3 88.9 all-gather.3
  117.8 47.1 all-gather.5
where the time goes:
time: 607 us; the launch traced here: 598 us
  other arithmetic  322 us (53%)
  waiting for transfers between devices  90.4 us (15%)
  local copies, waits for them, and re-layouts  88 us (14%)
  matrix products  64 us (11%)
  between operations  20.1 us (3%)
  blocking collectives  13.4 us (2%)
    another operation x30, other arithmetic, local(): factor = jnp.linalg.cholesky(symmetric)  173 us
    all_gather x1, waiting for transfers between devices, local(): gathered = lax.all_gather(packed, 'wide', axis=0, tiled=True)  90.4 us
    another operation x3, other arithmetic, lower_inverse(): lax.linalg.triangular_solve(lower_factor, identity, left_side=True, lower...  85.4 us
    another operation x14, matrix products, local(): factor = jnp.linalg.cholesky(symmetric)  23.1 us
    another operation x24, local copies, waits for them, and re-layouts  23 us
    another operation x15, matrix products, lower_inverse(): lax.linalg.triangular_solve(lower_factor, identity, left_side=True, lower...  22.2 us
    gather x3, other arithmetic, local(): first_flags = fill_pattern[0][block_ids]  20.6 us
    gather x2, other arithmetic, local(): second_flags = fill_pattern[1][block_ids]  19.9 us
  transfers between devices with their start and end apart: 2, of which 1 were waited for; matrix products, arithmetic and copies ran while one was open for 13% of the time, Pallas kernels for 0%

commit v1 on v0

--- a/solution.py
+++ b/solution.py
@@ -2,6 +2,7 @@
 import jax.numpy as jnp
 from jax import lax
 from jax.sharding import PartitionSpec as P
+from jax.lax import all_to_all, axis_size
 
 BLOCK = 256
 highest = lax.Precision.HIGHEST
@@ -18,6 +19,15 @@
 
 
 def local(assembled, row_map, fill_pattern, trailing_block):
+
+    def lay_squares_on_mesh(local_x, mesh_dim):
+        shelf = []
+        for _ in range(axis_size(mesh_dim)):
+            shelf.append(local_x)
+        state_now = all_to_all(jnp.stack(shelf, axis=0), mesh_dim, 0, 0)
+        lower = jnp.concatenate(state_now, axis=0)
+        return lower
+
     wide_count = lax.axis_size("wide")
     col_count = lax.axis_size("col")
     asm_rows, twice_width = assembled.shape
@@ -38,7 +48,7 @@
         ],
         axis=0,
     )
-    gathered = lax.all_gather(packed, "wide", axis=0, tiled=True)
+    gathered = lay_squares_on_mesh(packed, "wide")
     gathered3 = gathered.reshape(wide_count, packed_rows, twice_width)
     ids = gathered3[:, asm_rows, :asm_rows].astype(jnp.int32).reshape(-1)
     source = (

time: 607 us -> 766 us (1.26)
  waiting for transfers between devices: 90.4 us -> 229 us
  starting transfers between devices: 0.08 us -> 12.4 us
    all_to_all x0 -> x1, waiting for transfers between devices: none -> 229 us  [lay_squares_on_mesh(): state_now = all_to_all(jnp.stack(shelf, axis=0), mesh_dim, 0, 0)]
    all_gather x1 -> x0, waiting for transfers between devices: 90.4 us -> none  [local(): gathered = lax.all_gather(packed, 'wide', axis=0, tiled=True)]
    all_to_all x0 -> x1, starting transfers between devices: none -> 12.3 us  [lay_squares_on_mesh(): state_now = all_to_all(jnp.stack(shelf, axis=0), mesh_dim, 0, 0)]
    another operation x24 -> x25, local copies, waits for them, and re-layouts: 23 us -> 28.2 us
  transfers between devices with their start and end apart: 2 -> 2, of which waited for: 1 -> 1; matrix products, arithmetic and copies ran while one was open for 13% -> 10% of each run, Pallas kernels for 0% -> 0%
where the time goes in v1:
time: 766 us; the launch traced here: 755 us
  other arithmetic  323 us (42%)
  waiting for transfers between devices  229 us (30%)
  local copies, waits for them, and re-layouts  92.2 us (12%)
  matrix products  64 us (8%)
  between operations  20.1 us (3%)
  blocking collectives  13.4 us (2%)
  starting transfers between devices  12.4 us (2%)
    all_to_all x1, waiting for transfers between devices, lay_squares_on_mesh(): state_now = all_to_all(jnp.stack(shelf, axis=0), mesh_dim, 0, 0)  229 us
    another operation x30, other arithmetic, local(): factor = jnp.linalg.cholesky(symmetric)  173 us
    another operation x3, other arithmetic, lower_inverse(): lax.linalg.triangular_solve(lower_factor, identity, left_side=True, lower...  85.4 us
    another operation x14, matrix products, local(): factor = jnp.linalg.cholesky(symmetric)  23.1 us
    another operation x24, local copies, waits for them, and re-layouts  23 us
    another operation x15, matrix products, lower_inverse(): lax.linalg.triangular_solve(lower_factor, identity, left_side=True, lower...  22.2 us
    gather x3, other arithmetic, local(): first_flags = fill_pattern[0][block_ids]  20.6 us
    gather x2, other arithmetic, local(): second_flags = fill_pattern[1][block_ids]  19.9 us
  transfers between devices with their start and end apart: 2, of which 1 were waited for; matrix products, arithmetic and copies ran while one was open for 10% of the time, Pallas kernels for 0%

profile of v1, /device:TPU:2, one launch (start us, length us, event | category | flops | bytes accessed | tf_op | source)
XLA Modules:
  0.0 754.9 jit_solution(9869255326954131240)
XLA Ops:
  8.9 5.2 stack.2
  14.1 12.3 %all-to-all-start = ((f32[64,40,1024]{2,1,0:T(8,128)}), f32[64,40,1024]{2,1,0:T(8,128)}, u32[]{:S(2)}, u32[]{:S(2)}) async-start(f32[64,40,1024]{2,1,0:T(8,128)} %stack.2), calls=%async_computation | async-start | bytes 20971520 | tf_op jit(solution)/shard_map/all_to_all | solution.py:27
  26.7 229.3 %all-to-all-done = f32[64,40,1024]{2,1,0:T(8,128)} async-done(((f32[64,40,1024]{2,1,0:T(8,128)}), f32[64,40,1024]{2,1,0:T(8,128)}, u32[]{:S(2)}, u32[]{:S(2)}) %all-to-all-start) | async-done | bytes 10485792 | tf_op jit(solution)/shard_map/all_to_all | solution.py:27
  258.7 9.0 %scatter_custom_fusion.1 = s32[256]{0:T(256)S(1)} fusion(s32[2304]{0:T(1024)S(1)} %get-tuple-element.25, s32[2304]{0:T(1024)S(1)} %reshape.470, s32[]{:T(128)} %copy.64), kind=kCustom, calls=%fused_computation.239 | custom fusion | bytes 1028 | tf_op jit(solution)/shard_map/scatter | solution.py:59
  267.7 5.6 gather_fusion.1
  277.7 4.6 compare_select_fusion.7
  283.2 2.5 fusion.23
  285.8 4.2 compare_select_fusion.8
  290.0 15.6 %select_select_fusion.1 = s32[2048]{0:T(1024)S(1)} fusion(pred[2048]{0:T(1024)(128)(4,1)S(1)} %get-tuple-element.51, pred[2048]{0:T(1024)(128)(4,1)S(1)} %get-tuple-element.50, pred[2048]{0:T(1024)(128)(4,1)S(1)} %get-tuple-element.49, pred[2048]{0:T(1024)(128)(4,1)S(1)} %get-tuple-element.48, pred[2048]{0:T(1024)(128)(4,1)S(1)} %get-tuple-element.47, ...), kind=kLoop, calls=%fused_computation.213 | loop fusion | flops 51200 | bytes 67684 | tf_op jit(solution)/shard_map/gather | solution.py:77
  305.7 15.5 %select_select_fusion.2 = s32[2048]{0:T(1024)S(1)} fusion(pred[2048]{0:T(1024)(128)(4,1)S(1)} %get-tuple-element.51, pred[2048]{0:T(1024)(128)(4,1)S(1)} %get-tuple-element.50, pred[2048]{0:T(1024)(128)(4,1)S(1)} %get-tuple-element.49, pred[2048]{0:T(1024)(128)(4,1)S(1)} %get-tuple-element.48, pred[2048]{0:T(1024)(128)(4,1)S(1)} %get-tuple-element.47, ...), kind=kLoop, calls=%fused_computation.214 | loop fusion | flops 51200 | bytes 67684 | tf_op jit(solution)/shard_map/gather | solution.py:76
  321.1 9.0 %scatter_custom_fusion = s32[2048]{0:T(1024)S(1)} fusion(s32[2304]{0:T(1024)S(1)} %get-tuple-element.26, s32[2304]{0:T(1024)S(1)} %reshape.470, s32[]{:T(128)} %copy.64), kind=kCustom, calls=%fused_computation.217 | custom fusion | bytes 8196 | tf_op jit(solution)/shard_map/scatter | solution.py:68
  330.1 15.7 %gather_fusion = f32[2048,1024]{1,0:T(8,128)} fusion(f32[2560,1024]{1,0:T(8,128)} %bitcast.1, s32[2048]{0:T(1024)S(1)} %fusion.75), kind=kCustom, calls=%fused_computation | custom fusion | bytes 16785408 | tf_op jit(solution)/shard_map/gather | solution.py:70
  345.9 5.4 convert_multiply_fusion
  351.3 3.2 copy-done
  354.5 13.4 %all_gather.6 = f32[128,1024]{1,0:T(8,128)S(1)} all-gather(f32[32,1024]{1,0:T(8,128)S(1)} %constant_dynamic-slice_fusion.2), channel_id=1, replica_groups=mesh['wide'=64,'col'=4] {'col'}, dimensions={0}, use_global_device_ids=true | all-gather | bytes 655360 | tf_op jit(solution)/shard_map/all_gather | solution.py:84
  367.9 5.4 copy.17
  373.2 6.8 fusion.1
  380.1 5.5 copy.18
  385.6 4.4 fusion
  390.0 2.0 copy-done.2
  392.0 11.7 %cholesky.223 = f32[128,128]{1,0:T(8,128)S(1)} custom-call(f32[128,128]{1,0:T(8,128)S(1)} %cholesky.580), custom_call_target="Cholesky" | custom-call | tf_op jit(solution)/shard_map/jit(cholesky)/cholesky | solution.py:86
  403.8 2.5 cholesky.255
  406.2 9.8 %custom-call.62 = f32[1,128,128]{1,2,0:T(8,128)S(1)} custom-call(f32[1,128,128]{2,1,0:T(8,128)S(1)} %get-tuple-element.112), custom_call_target="InvertDiagBlocksLowerTriangular" | custom-call | tf_op jit(solution)/shard_map/jit(cholesky)/cholesky | solution.py:86
  416.0 2.3 constant_dynamic-update-slice_fusion.30
  420.0 12.1 %cholesky.244 = f32[128,128]{1,0:T(8,128)S(1)} custom-call(f32[128,128]{1,0:T(8,128)S(1)} %cholesky.584), custom_call_target="Cholesky" | custom-call | tf_op jit(solution)/shard_map/jit(cholesky)/cholesky | solution.py:86
  432.7 9.8 %custom-call.63 = f32[1,128,128]{1,2,0:T(8,128)S(1)} custom-call(f32[1,128,128]{2,1,0:T(8,128)S(1)} %get-tuple-element.109), custom_call_target="InvertDiagBlocksLowerTriangular" | custom-call | tf_op jit(solution)/shard_map/jit(cholesky)/cholesky | solution.py:86
  443.8 2.1 convolution_subtract_fusion.6
  445.9 11.7 %cholesky.468 = f32[128,128]{1,0:T(8,128)S(1)} custom-call(f32[128,128]{1,0:T(8,128)S(1)} %cholesky.589), custom_call_target="Cholesky" | custom-call | tf_op jit(solution)/shard_map/jit(cholesky)/cholesky | solution.py:86
  458.9 9.8 %custom-call.64 = f32[1,128,128]{1,2,0:T(8,128)S(1)} custom-call(f32[1,128,128]{2,1,0:T(8,128)S(1)} %get-tuple-element.106), custom_call_target="InvertDiagBlocksLowerTriangular" | custom-call | tf_op jit(solution)/shard_map/jit(cholesky)/cholesky | solution.py:86
  469.9 2.3 convolution_subtract_fusion.7
  472.3 11.8 %cholesky.487 = f32[128,128]{1,0:T(8,128)S(1)} custom-call(f32[128,128]{1,0:T(8,128)S(1)} %cholesky.594), custom_call_target="Cholesky" | custom-call | tf_op jit(solution)/shard_map/jit(cholesky)/cholesky | solution.py:86
  485.4 9.8 %custom-call.65 = f32[1,128,128]{1,2,0:T(8,128)S(1)} custom-call(f32[1,128,128]{2,1,0:T(8,128)S(1)} %get-tuple-element.103), custom_call_target="InvertDiagBlocksLowerTriangular" | custom-call | tf_op jit(solution)/shard_map/jit(cholesky)/cholesky | solution.py:86
  496.3 2.3 convolution_subtract_fusion.8
  498.7 11.7 %cholesky.506 = f32[128,128]{1,0:T(8,128)S(1)} custom-call(f32[128,128]{1,0:T(8,128)S(1)} %cholesky.599), custom_call_target="Cholesky" | custom-call | tf_op jit(solution)/shard_map/jit(cholesky)/cholesky | solution.py:86
  511.7 10.0 %custom-call.66 = f32[1,128,128]{1,2,0:T(8,128)S(1)} custom-call(f32[1,128,128]{2,1,0:T(8,128)S(1)} %get-tuple-element.100), custom_call_target="InvertDiagBlocksLowerTriangular" | custom-call | tf_op jit(solution)/shard_map/jit(cholesky)/cholesky | solution.py:86
  522.7 2.3 convolution_subtract_fusion.9
  525.0 11.7 %cholesky.526 = f32[128,128]{1,0:T(8,128)S(1)} custom-call(f32[128,128]{1,0:T(8,128)S(1)} %cholesky.604), custom_call_target="Cholesky" | custom-call | tf_op jit(solution)/shard_map/jit(cholesky)/cholesky | solution.py:86
  538.0 9.8 %custom-call.67 = f32[1,128,128]{1,2,0:T(8,128)S(1)} custom-call(f32[1,128,128]{2,1,0:T(8,128)S(1)} %get-tuple-element.97), custom_call_target="InvertDiagBlocksLowerTriangular" | custom-call | tf_op jit(solution)/shard_map/jit(cholesky)/cholesky | solution.py:86
  548.8 2.1 convolution_subtract_fusion.10
  550.9 12.1 %cholesky.546 = f32[128,128]{1,0:T(8,128)S(1)} custom-call(f32[128,128]{1,0:T(8,128)S(1)} %cholesky.609), custom_call_target="Cholesky" | custom-call | tf_op jit(solution)/shard_map/jit(cholesky)/cholesky | solution.py:86
  564.3 9.8 %custom-call.68 = f32[1,128,128]{1,2,0:T(8,128)S(1)} custom-call(f32[1,128,128]{2,1,0:T(8,128)S(1)} %get-tuple-element.94), custom_call_target="InvertDiagBlocksLowerTriangular" | custom-call | tf_op jit(solution)/shard_map/jit(cholesky)/cholesky | solution.py:86
  575.0 1.8 convolution_subtract_fusion.11
  576.7 11.7 %cholesky.564 = f32[128,128]{1,0:T(8,128)S(1)} custom-call(f32[128,128]{1,0:T(8,128)S(1)} %convolution_subtract_fusion.11), custom_call_target="Cholesky" | custom-call | tf_op jit(solution)/shard_map/jit(cholesky)/cholesky | solution.py:86
  595.4 6.6 fusion.2
  602.0 23.2 %while.2 = (s32[]{:T(128)}, f32[1024,1024]{1,0:T(8,128)}, s32[8,2]{0,1:T(2,128)S(1)}, f32[8,128,128]{2,1,0:T(8,128)S(1)}, s32[]{:T(128)}) while((s32[]{:T(128)}, f32[1024,1024]{1,0:T(8,128)}, s32[8,2]{0,1:T(2,128)S(1)}, f32[8,128,128]{2,1,0:T(8,128)S(1)}, s32[]{:T(128)}) %tuple.153), condition=%wide.while_cond.1, body=%wide.while_body.1.sunk | while | flops 2 | bytes 131189 | solution.py:14
  602.6 2.3 bitcast_dynamic-update-slice_fusion.2
  605.5 2.3 bitcast_dynamic-update-slice_fusion.2
  608.4 2.3 bitcast_dynamic-update-slice_fusion.2
  611.3 2.3 bitcast_dynamic-update-slice_fusion.2
  614.2 2.3 bitcast_dynamic-update-slice_fusion.2
  617.1 2.3 bitcast_dynamic-update-slice_fusion.2
  620.0 2.3 bitcast_dynamic-update-slice_fusion.2
  622.9 2.2 bitcast_dynamic-update-slice_fusion.2
  625.2 78.8 %custom-call.69 = f32[8,128,128]{1,2,0:T(8,128)S(1)} custom-call(f32[8,128,128]{2,1,0:T(8,128)S(1)} %get-tuple-element.22), custom_call_target="InvertDiagBlocksLowerTriangular" | custom-call | tf_op jit(solution)/shard_map/triangular_solve | solution.py:14
  704.5 1.9 convolution_subtract_fusion.4
  709.6 2.0 fusion.17
  712.4 2.2 fusion.20
  715.3 2.6 convolution_subtract_fusion.2
  718.7 2.8 convolution_subtract_fusion.1
  722.1 3.5 convolution_subtract_fusion.3
  726.3 4.6 fusion.91
  730.9 4.5 fusion.88
  735.3 2.4 fusion.89
  737.8 7.3 fusion.90
  (103 shorter events, 41.4 us)
Async XLA Ops:
  14.1 241.9 %all-to-all-start = ((f32[64,40,1024]{2,1,0:T(8,128)}), f32[64,40,1024]{2,1,0:T(8,128)}, u32[]{:S(2)}, u32[]{:S(2)}) async-start(f32[64,40,1024]{2,1,0:T(8,128)} %stack.2), calls=%async_computation | async-start | bytes 20971520 | tf_op jit(solution)/shard_map/all_to_all | solution.py:27
  26.4 341.4 %all-gather.3.cloned.1.call-start = ((), (), s32[]{:S(2)}) async-start(), calls=%async_computation.1 | async-start | bytes 5242880 | tf_op jit(solution)/shard_map/all_gather | solution.py:61
  267.7 7.1 copy-start.4
  351.3 3.2 copy-start
  390.0 2.0 copy-start.2
  703.9 3.2 copy-start.1
  725.6 12.1 %slice-start = ((s8[8388608]{0:T(1024)(128)(4,1)}), s8[4194304]{0:T(1024)(128)(4,1)S(1)}, s32[]{:S(2)}) async-start(s8[8388608]{0:T(1024)(128)(4,1)} %bitcast.187), calls=%async_computation.2 | async-start | bytes 8388608
  730.9 6.9 slice-start.1
  737.8 8.7 %copy-start.3 = (f32[64,1,32,128]{3,2,1,0:T(8,128)S(1)}, f32[64,1,32,128]{3,2,1,0:T(8,128)}, u32[]{:S(2)}) copy-start(f32[64,1,32,128]{3,2,1,0:T(8,128)} %param.9) | copy-start | bytes 3145732
Sparse Core Ops, SparseCore 0:
  274.7 47.8 all-gather.2
